TPU v7x, 256 devices: a whole 4x4x8 slice. The times are simulated.
256 devices in a mesh: seq: 8 (over z_lo, x), chan: 32 (over y, z_hi, core).
Axes of the slice: x: 4, y: 4, z: 8 (z_hi: 4, z_lo: 2; z = z_hi * 2 + z_lo), core: 2. Of those that a mesh axis runs over, the one named last changes fastest.
Arguments:
- tokens: bfloat16 [8192, 4096], P('seq', 'chan'), may hold values from -6 to 6
- in_weight: bfloat16 [4096, 3, 4096], P(None, None, 'chan'), may hold values from -0.09375 to 0.09375
- short_taps: float32 [3, 3, 4096], P(None, None, 'chan'), may hold values from -3 to 3
- filter_taps: float32 [8192, 4096], P('seq', 'chan'), may hold values from -1 to 1
- skip_gain: float32 [4096], P('chan'), may hold values from -4 to 4
- out_weight: bfloat16 [4096, 4096], P('chan'), may hold values from -0.1875 to 0.1875
Outputs:
- layer_out: bfloat16 [8192, 4096], P('seq', 'chan')
All inputs are finite; a program needn't handle non-finite values.
Results may differ from a plain program's by a relative error of at most 0.007.
Values may be sent and summed in bfloat16 or wider, within the bound.
No kernel may reach another device: no remote copies, remote signals or barrier semaphores. Data moves between devices by JAX's collectives and lax.ppermute only.
A program may use at most 128 MiB of HBM per device.

v0:
```python
import math
import jax
import jax.numpy as jnp
from jax import lax
from jax.sharding import PartitionSpec as P

COLS = 256
highest = lax.Precision.HIGHEST


def from_behind(shard, axis, by):
    size = lax.axis_size(axis)
    pairs = [(i, i + by) for i in range(size) if 0 <= i + by < size]
    return lax.ppermute(shard, axis, pairs)


def phase_table(row_count, col_count, period):
    row_index = jnp.arange(row_count, dtype=jnp.int32)[:, None]
    col_index = jnp.arange(col_count, dtype=jnp.int32)[None, :]
    angle = (row_index * col_index % period).astype(jnp.float32) * (2.0 * math.pi / period)
    return (jnp.cos(angle), jnp.sin(angle))


def real_transform(signal, cosine, sines, pattern):
    real_part = jnp.einsum(pattern, cosine, signal, precision=highest)
    imag_part = -jnp.einsum(pattern, sines, signal, precision=highest)
    return (real_part, imag_part)


def complex_transform(real_part, imag_part, cosine, sines, direction, pattern):
    cos_real = jnp.einsum(pattern, cosine, real_part, precision=highest)
    cos_imag = jnp.einsum(pattern, cosine, imag_part, precision=highest)
    sin_real = jnp.einsum(pattern, sines, real_part, precision=highest)
    sin_imag = jnp.einsum(pattern, sines, imag_part, precision=highest)
    return (cos_real - direction * sin_imag, cos_imag + direction * sin_real)


def rotate(real_part, imag_part, cosine, sines, direction):
    return (
        real_part * cosine - direction * imag_part * sines,
        imag_part * cosine + direction * real_part * sines,
    )


def spectrum_product(real_part, imag_part):
    prod_real = real_part[0] * real_part[1] - imag_part[0] * imag_part[1]
    prod_imag = real_part[0] * imag_part[1] + imag_part[0] * real_part[1]
    return (prod_real[None], prod_imag[None])


def real_inverse(real_part, imag_part, cosine, sines, pattern, length):
    return (
        jnp.einsum(pattern, cosine, real_part, precision=highest)
        - jnp.einsum(pattern, sines, imag_part, precision=highest)
    ) / length


def channel_convolve(signal, filter_taps):
    stacked = jnp.stack([signal, filter_taps])
    whole_seq = lax.all_to_all(stacked, "seq", split_axis=2, concat_axis=1, tiled=True)
    length = whole_seq.shape[1]
    narrow = whole_seq.shape[2]
    full_rows = 2 * length // COLS
    half_rows = full_rows // 2
    period = 2 * length
    laid_out = whole_seq.reshape(2, half_rows, COLS, narrow)
    first_cos, first_sin = phase_table(full_rows, half_rows, full_rows)
    real_part, imag_part = real_transform(laid_out, first_cos, first_sin, "kn,xnmc->xkmc")
    twist_cos, twist_sin = phase_table(full_rows, COLS, period)
    twist_cos = twist_cos[:, :, None]
    twist_sin = twist_sin[:, :, None]
    real_part, imag_part = rotate(real_part, imag_part, twist_cos, twist_sin, -1.0)
    second_cos, second_sin = phase_table(COLS, COLS, COLS)
    pattern = "kn,xanc->xakc"
    real_part, imag_part = complex_transform(
        real_part, imag_part, second_cos, second_sin, -1.0, pattern
    )
    real_part, imag_part = spectrum_product(real_part, imag_part)
    real_part, imag_part = complex_transform(
        real_part, imag_part, second_cos, second_sin, 1.0, pattern
    )
    real_part, imag_part = rotate(real_part, imag_part, twist_cos, twist_sin, 1.0)
    last_cos, last_sin = phase_table(half_rows, full_rows, full_rows)
    values = real_inverse(real_part, imag_part, last_cos, last_sin, "nk,xkmc->xnmc", period)
    values = values.reshape(length, narrow)
    return lax.all_to_all(values, "seq", split_axis=0, concat_axis=1, tiled=True)


def body(tokens, in_weight, short_taps, filter_taps, skip_gain, out_weight):
    tok_count = tokens.shape[0]
    chan_count = in_weight.shape[2]
    flat_weight = in_weight.reshape(in_weight.shape[0], 3 * chan_count)
    projected = jnp.dot(
        lax.all_gather(tokens, "chan", axis=1, tiled=True),
        flat_weight,
        preferred_element_type=jnp.float32,
    )
    projected = projected.astype(jnp.bfloat16).reshape(tok_count, 3, chan_count)
    previous = from_behind(projected[-2:], "seq", 1)
    extended = jnp.concatenate([previous, projected], axis=0).astype(jnp.float32)
    short_mixed = (
        short_taps[0] * extended[2:]
        + short_taps[1] * extended[1:-1]
        + short_taps[2] * extended[:-2]
    )
    gate_out = short_mixed[:, 0]
    signal = short_mixed[:, 1] * short_mixed[:, 2]
    convolved = channel_convolve(signal, filter_taps)
    hidden = (gate_out * (convolved + skip_gain * signal)).astype(jnp.bfloat16)
    partial_terms = jnp.dot(hidden, out_weight, preferred_element_type=jnp.float32)
    layer_out = lax.psum_scatter(partial_terms, "chan", scatter_dimension=1, tiled=True)
    return layer_out.astype(jnp.bfloat16)


def solution(mesh):
    in_specs = (
        P("seq", "chan"),
        P(None, None, "chan"),
        P(None, None, "chan"),
        P("seq", "chan"),
        P("chan"),
        P("chan", None),
    )
    out_specs = P("seq", "chan")
    return jax.shard_map(body, mesh=mesh, in_specs=in_specs, out_specs=out_specs, check_vma=False)
```

profile of v0, /device:TPU:6, one launch (start us, length us, event | category | flops | bytes accessed | tf_op | source)
XLA Modules:
  0.0 368.0 jit_solution(10557821155383948905)
XLA Ops:
  6.5 0.7 all-gather.2.cloned.1.call-update
  7.3 4.8 %copy.29 = bf16[4096,3,128]{0,2,1:T(8,128)(2,1)} copy(bf16[4096,3,128]{2,0,1:T(8,128)(2,1)} %param.7) | data formatting | bytes 6291456 | tf_op args[1]
  12.0 84.9 %all-gather.2.cloned.1.call-done = bf16[1024,4096]{1,0:T(8,128)(2,1)} async-done(((bf16[1024,128]{1,0:T(8,128)(2,1)}), bf16[1024,4096]{1,0:T(8,128)(2,1)}) %all-gather.2.cloned.1.call-update) | async-done | bytes 8388624 | tf_op jit(solution)/shard_map/all_gather | solution.py:94
  97.0 8.8 %convolution_convert_fusion = bf16[1024,384]{1,0:T(8,128)(2,1)S(1)} fusion(bf16[1024,4096]{1,0:T(8,128)(2,1)} %all-gather.2.cloned.1.call-done, bf16[4096,384]{0,1:T(8,128)(2,1)} %bitcast.137), kind=kOutput, calls=%fused_computation.21 | convolution fusion | flops 3221618688 | bytes 12320768 | tf_op jit(solution)/shard_map/dot_general | solution.py:93
  105.8 1.9 collective-permute-start
  108.3 3.0 collective-permute-done
  111.9 1.2 fusion.14
  113.2 1.8 copy.33
  115.0 4.8 %all-to-all-start = ((f32[2,1024,128]{1,0,2:T(2,128)}), f32[2,1024,128]{1,0,2:T(2,128)}, u32[]{:S(2)}, u32[]{:S(2)}) async-start(f32[2,1024,128]{1,0,2:T(2,128)} %copy.33), calls=%async_computation | async-start | bytes 2097152 | tf_op jit(solution)/shard_map/all_to_all | solution.py:60
  119.8 0.5 reduce-scatter.2.cloned.1.call-start
  120.8 11.4 %all-to-all-done = f32[2,1024,128]{1,0,2:T(2,128)} async-done(((f32[2,1024,128]{1,0,2:T(2,128)}), f32[2,1024,128]{1,0,2:T(2,128)}, u32[]{:S(2)}, u32[]{:S(2)}) %all-to-all-start) | async-done | bytes 1048608 | tf_op jit(solution)/shard_map/all_to_all | solution.py:60
  132.3 1.6 copy.34
  133.8 1.6 copy.35
  135.4 2.5 reshape.85
  137.9 3.2 fusion.70
  141.2 2.4 fusion
  143.6 3.8 %fusion.2 = f32[2,64,16,256]{3,2,1,0:T(8,128)S(1)} fusion(f32[2,64,256,16]{2,1,3,0:T(8,128)S(1)} %get-tuple-element.6), kind=kOutput, calls=%fused_computation.8 | convolution fusion | flops 1611530240 | bytes 4194304 | tf_op jit(solution)/shard_map/kn,xanc->xakc/dot_general | solution.py:32
  147.4 4.0 %fusion.4 = f32[2,64,16,256]{3,2,1,0:T(8,128)S(1)} fusion(f32[2,64,256,16]{2,1,3,0:T(8,128)S(1)} %get-tuple-element.6), kind=kOutput, calls=%fused_computation.10 | convolution fusion | flops 1611530240 | bytes 4194304 | tf_op jit(solution)/shard_map/kn,xanc->xakc/dot_general | solution.py:34
  151.4 3.9 %subtract_bitcast_fusion = f32[2,64,256,16]{2,3,1,0:T(8,128)S(1)} fusion(f32[2,64,16,256]{3,2,1,0:T(8,128)S(1)} %fusion.4, f32[2,64,256,16]{2,1,3,0:T(8,128)S(1)} %get-tuple-element.5), kind=kOutput, calls=%fused_computation.7 | convolution fusion | flops 1612578816 | bytes 6291456 | tf_op jit(solution)/shard_map/kn,xanc->xakc/dot_general | solution.py:31
  155.4 3.9 %add_bitcast_fusion = f32[2,64,256,16]{2,3,1,0:T(8,128)S(1)} fusion(f32[2,64,16,256]{3,2,1,0:T(8,128)S(1)} %fusion.2, f32[2,64,256,16]{2,1,3,0:T(8,128)S(1)} %get-tuple-element.5), kind=kOutput, calls=%fused_computation.6 | convolution fusion | flops 1612578816 | bytes 6291456 | tf_op jit(solution)/shard_map/kn,xanc->xakc/dot_general | solution.py:33
  159.2 0.6 multiply_subtract_fusion
  159.8 2.0 fusion.24
  161.8 2.2 fusion.20
  164.0 2.0 fusion.16
  166.0 2.1 add_bitcast_fusion.1
  168.1 1.3 fusion.27
  169.5 2.1 fusion.19
  171.6 1.2 all_to_all.28
  173.1 12.9 %all_to_all.34 = f32[8,1024,16]{1,2,0:T(8,128)S(1)} all-to-all(f32[8,1024,16]{1,2,0:T(8,128)S(1)} %copy.42), channel_id=1, replica_groups=mesh['seq'=8,'chan'=32] {'seq'}, dimensions={0} | all-to-all | bytes 1048576 | tf_op jit(solution)/shard_map/all_to_all | solution.py:86
  186.2 8.1 %fusion.142 = f32[1024,4096]{1,0:T(8,128)} fusion(bf16[1024,128]{0,1:T(8,128)(2,1)S(1)} %fusion.30, bf16[128,4096]{1,0:T(8,128)(2,1)S(1)} %copy-done), kind=kOutput, calls=%fused_computation.161 | convolution fusion | flops 1073741824 | bytes 18087936 | tf_op jit(solution)/shard_map/dot_general | solution.py:110
  194.4 164.8 %reduce-scatter.2.cloned.1.call-done = f32[1024,128]{1,0:T(8,128)} async-done(((f32[1024,4096]{1,0:T(8,128)}), f32[1024,128]{1,0:T(8,128)}) %reduce-scatter.2.cloned.1.call-update) | async-done | bytes 524304 | tf_op jit(solution)/shard_map/reduce_scatter | solution.py:111
  359.2 1.8 convert_element_type.67
  (25 shorter events, 2.2 us)
Async XLA Ops:
  6.5 179.7 %copy-start = (bf16[128,4096]{1,0:T(8,128)(2,1)S(1)}, bf16[128,4096]{1,0:T(8,128)(2,1)}, u32[]{:S(2)}) copy-start(bf16[128,4096]{1,0:T(8,128)(2,1)} %param.11) | copy-start | bytes 3145732
  6.5 90.4 %all-gather.2.cloned.1.call-start = ((), (), s32[]{:S(2)}) async-start(), calls=%async_computation.3 | async-start | bytes 8650752 | tf_op jit(solution)/shard_map/all_gather | solution.py:94
  97.0 10.8 %copy-start.3 = (f32[3,3,128]{2,1,0:T(4,128)S(1)}, f32[3,3,128]{2,1,0:T(4,128)}, u32[]{:S(2)}) copy-start(f32[3,3,128]{2,1,0:T(4,128)} %param.8) | copy-start | bytes 13828
  97.0 10.8 %copy-start.2 = (f32[1024,128]{1,0:T(8,128)S(1)}, f32[1024,128]{1,0:T(8,128)}, u32[]{:S(2)}) copy-start(f32[1024,128]{1,0:T(8,128)} %param.9) | copy-start | bytes 1572868
  105.8 5.5 %collective-permute-start = (bf16[2,3,128]{2,1,0:T(4,128)(2,1)S(1)}, bf16[2,3,128]{2,1,0:T(4,128)(2,1)S(1)}, u32[]{:S(2)}, u32[]{:S(2)}) collective-permute-start(bf16[2,3,128]{2,1,0:T(4,128)(2,1)S(1)} %slice.51), channel_id=1, source_target_pairs={{0,32},{32,64},{64,96},{96,128},{128,160},{160,192},{192,224},{1,3... | collective-permute-start | bytes 4616 | tf_op jit(solution)/shard_map/ppermute | solution.py:14
  115.0 17.3 %all-to-all-start = ((f32[2,1024,128]{1,0,2:T(2,128)}), f32[2,1024,128]{1,0,2:T(2,128)}, u32[]{:S(2)}, u32[]{:S(2)}) async-start(f32[2,1024,128]{1,0,2:T(2,128)} %copy.33), calls=%async_computation | async-start | bytes 2097152 | tf_op jit(solution)/shard_map/all_to_all | solution.py:60
  119.8 239.3 %reduce-scatter.2.cloned.1.call-start = ((), (), s32[]{:S(2)}) async-start(), calls=%async_computation.4 | async-start | bytes 17301504 | tf_op jit(solution)/shard_map/reduce_scatter | solution.py:111
  137.9 3.2 copy-start.1
  171.6 14.5 %copy-start.4 = (f32[128]{0:T(128)S(1)}, f32[128]{0:T(128)}, u32[]{:S(2)}) copy-start(f32[128]{0:T(128)} %param.10) | copy-start | bytes 1540
Sparse Core Ops, SparseCore 0:
  9.8 87.1 all-gather.1
  194.5 164.6 reduce-scatter.1
where the time goes:
time: 374 us; the launch traced here: 368 us
  waiting for transfers between devices  265 us (71%)
  matrix products  49.9 us (13%)
  local copies, waits for them, and re-layouts  14.5 us (4%)
  between operations  13.8 us (4%)
  blocking collectives  12.9 us (3%)
  starting transfers between devices  7.19 us (2%)
  other arithmetic  4.7 us (1%)
    reduce_scatter x1, waiting for transfers between devices, body(): lax.psum_scatter(partial_terms, 'chan', scatter_dimension=1, tiled=True)  165 us
    all_gather x1, waiting for transfers between devices, body(): lax.all_gather(tokens, 'chan', axis=1, tiled=True)  84.9 us
    all_to_all x1, blocking collectives, channel_convolve(): lax.all_to_all(values, 'seq', split_axis=0, concat_axis=1, tiled=True)  12.9 us
    all_to_all x1, waiting for transfers between devices, channel_convolve(): lax.all_to_all(stacked, 'seq', split_axis=2, concat_axis=1, tiled=True)  11.4 us
    dot_general x1, matrix products, body(): jnp.dot(lax.all_gather(tokens, 'chan', axis=1, tiled=True), flat_weight,...  8.84 us
    dot_general x1, matrix products, body(): jnp.dot(hidden, out_weight, preferred_element_type=jnp.float32)  8.12 us
  transfers between devices with their start and end apart: 4, of which 4 were waited for; matrix products, arithmetic and copies ran while one was open for 2% of the time, Pallas kernels for 0%

commit v1 on v0

--- a/solution.py
+++ b/solution.py
@@ -6,6 +6,9 @@
 
 COLS = 256
 highest = lax.Precision.HIGHEST
+mix_masks_on_mesh = lambda point: jnp.concatenate(
+    lax.all_to_all(jnp.stack(lax.axis_size("chan") * [point]), "chan", 0, 0), axis=1
+)
 
 
 def from_behind(shard, axis, by):
@@ -90,11 +93,7 @@
     tok_count = tokens.shape[0]
     chan_count = in_weight.shape[2]
     flat_weight = in_weight.reshape(in_weight.shape[0], 3 * chan_count)
-    projected = jnp.dot(
-        lax.all_gather(tokens, "chan", axis=1, tiled=True),
-        flat_weight,
-        preferred_element_type=jnp.float32,
-    )
+    projected = jnp.dot(mix_masks_on_mesh(tokens), flat_weight, preferred_element_type=jnp.float32)
     projected = projected.astype(jnp.bfloat16).reshape(tok_count, 3, chan_count)
     previous = from_behind(projected[-2:], "seq", 1)
     extended = jnp.concatenate([previous, projected], axis=0).astype(jnp.float32)

time: 374 us -> 487 us (1.30)
  waiting for transfers between devices: 265 us -> 351 us
  starting transfers between devices: 7.19 us -> 27.3 us
  local copies, waits for them, and re-layouts: 14.5 us -> 19.9 us
    all_to_all x0 -> x1, waiting for transfers between devices: none -> 177 us  [lax.all_to_all(jnp.stack(lax.axis_size('chan') * [point]), 'chan', 0, 0)]
    all_gather x1 -> x0, waiting for transfers between devices: 84.9 us -> none  [body(): lax.all_gather(tokens, 'chan', axis=1, tiled=True)]
    all_to_all x0 -> x1, starting transfers between devices: none -> 11.6 us  [lax.all_to_all(jnp.stack(lax.axis_size('chan') * [point]), 'chan', 0, 0)]
    ppermute x1, starting transfers between devices: 1.92 us -> 8.62 us  [from_behind(): return lax.ppermute(shard, axis, pairs)]
  transfers between devices with their start and end apart: 4 -> 4, of which waited for: 4 -> 4; matrix products, arithmetic and copies ran while one was open for 2% -> 1% of each run, Pallas kernels for 0% -> 0%
where the time goes in v1:
time: 487 us; the launch traced here: 480 us
  waiting for transfers between devices  351 us (72%)
  matrix products  50 us (10%)
  starting transfers between devices  27.3 us (6%)
  local copies, waits for them, and re-layouts  19.9 us (4%)
  between operations  13.9 us (3%)
  blocking collectives  12.6 us (3%)
    all_to_all x1, waiting for transfers between devices, lax.all_to_all(jnp.stack(lax.axis_size('chan') * [point]), 'chan', 0, 0)  177 us
    reduce_scatter x1, waiting for transfers between devices, body(): lax.psum_scatter(partial_terms, 'chan', scatter_dimension=1, tiled=True)  163 us
    all_to_all x1, blocking collectives, channel_convolve(): lax.all_to_all(values, 'seq', split_axis=0, concat_axis=1, tiled=True)  12.6 us
    all_to_all x1, starting transfers between devices, lax.all_to_all(jnp.stack(lax.axis_size('chan') * [point]), 'chan', 0, 0)  11.6 us
    all_to_all x1, waiting for transfers between devices, channel_convolve(): lax.all_to_all(stacked, 'seq', split_axis=2, concat_axis=1, tiled=True)  10.7 us
  transfers between devices with their start and end apart: 4, of which 4 were waited for; matrix products, arithmetic and copies ran while one was open for 1% of the time, Pallas kernels for 0%

profile of v1, /device:TPU:6, one launch (start us, length us, event | category | flops | bytes accessed | tf_op | source)
XLA Modules:
  0.0 479.6 jit_solution(145103597572445957)
XLA Ops:
  6.5 1.2 copy.30
  7.7 4.3 stack.6
  12.0 11.6 %all-to-all-start = ((bf16[32,1024,128]{1,2,0:T(8,128)(2,1)}), bf16[32,1024,128]{1,2,0:T(8,128)(2,1)}, u32[]{:S(2)}, u32[]{:S(2)}) async-start(bf16[32,1024,128]{1,2,0:T(8,128)(2,1)} %stack.6), calls=%async_computation | async-start | bytes 16777216 | tf_op jit(solution)/shard_map/all_to_all | solution.py:10
  23.7 4.7 copy.31
  28.4 177.3 %all-to-all-done = bf16[32,1024,128]{1,2,0:T(8,128)(2,1)} async-done(((bf16[32,1024,128]{1,2,0:T(8,128)(2,1)}), bf16[32,1024,128]{1,2,0:T(8,128)(2,1)}, u32[]{:S(2)}, u32[]{:S(2)}) %all-to-all-start) | async-done | bytes 8388640 | tf_op jit(solution)/shard_map/all_to_all | solution.py:10
  205.7 8.9 %convolution_convert_fusion = bf16[1024,384]{1,0:T(8,128)(2,1)S(1)} fusion(bf16[1024,4096]{0,1:T(8,128)(2,1)} %bitcast.2, bf16[4096,384]{0,1:T(8,128)(2,1)} %bitcast.140), kind=kOutput, calls=%fused_computation.21 | convolution fusion | flops 3221618688 | bytes 12320768 | tf_op jit(solution)/shard_map/dot_general | solution.py:96
  214.6 8.6 %collective-permute-start = (bf16[2,3,128]{2,1,0:T(4,128)(2,1)S(1)}, bf16[2,3,128]{2,1,0:T(4,128)(2,1)S(1)}, u32[]{:S(2)}, u32[]{:S(2)}) collective-permute-start(bf16[2,3,128]{2,1,0:T(4,128)(2,1)S(1)} %slice.51), channel_id=1, source_target_pairs={{0,32},{32,64},{64,96},{96,128},{128,160},{160,192},{192,224},{1,3... | collective-permute-start | bytes 4616 | tf_op jit(solution)/shard_map/ppermute | solution.py:17
  223.8 0.8 collective-permute-done
  225.1 1.2 fusion.14
  226.4 1.8 copy.35
  228.2 6.6 %all-to-all-start.1 = ((f32[2,1024,128]{1,0,2:T(2,128)}), f32[2,1024,128]{1,0,2:T(2,128)}, u32[]{:S(2)}, u32[]{:S(2)}) async-start(f32[2,1024,128]{1,0,2:T(2,128)} %copy.35), calls=%async_computation.1 | async-start | bytes 2097152 | tf_op jit(solution)/shard_map/all_to_all | solution.py:63
  235.8 10.7 %all-to-all-done.1 = f32[2,1024,128]{1,0,2:T(2,128)} async-done(((f32[2,1024,128]{1,0,2:T(2,128)}), f32[2,1024,128]{1,0,2:T(2,128)}, u32[]{:S(2)}, u32[]{:S(2)}) %all-to-all-start.1) | async-done | bytes 1048608 | tf_op jit(solution)/shard_map/all_to_all | solution.py:63
  246.5 1.6 copy.36
  248.1 1.6 copy.37
  249.7 2.5 reshape.95
  252.2 3.2 fusion.70
  255.4 2.4 fusion
  257.8 3.9 fusion.4
  261.7 4.0 fusion.2
  265.7 3.9 subtract_bitcast_fusion
  269.7 3.9 add_bitcast_fusion
  274.0 2.0 fusion.20
  276.0 2.2 fusion.24
  278.2 2.0 fusion.16
  280.2 2.1 add_bitcast_fusion.1
  282.4 1.3 fusion.27
  283.7 2.1 fusion.19
  285.8 1.2 all_to_all.32
  287.3 12.6 %all_to_all.39 = f32[8,1024,16]{1,2,0:T(8,128)S(1)} all-to-all(f32[8,1024,16]{1,2,0:T(8,128)S(1)} %copy.44), channel_id=1, replica_groups=mesh['seq'=8,'chan'=32] {'seq'}, dimensions={0} | all-to-all | bytes 1048576 | tf_op jit(solution)/shard_map/all_to_all | solution.py:89
  300.1 8.1 %fusion.142 = f32[1024,4096]{1,0:T(8,128)} fusion(bf16[1024,128]{0,1:T(8,128)(2,1)S(1)} %fusion.30, bf16[128,4096]{1,0:T(8,128)(2,1)S(1)} %copy-done), kind=kOutput, calls=%fused_computation.161 | convolution fusion | flops 1073741824 | bytes 18087936 | tf_op jit(solution)/shard_map/dot_general | solution.py:109
  308.2 162.5 %reduce-scatter.2.cloned.1.call-done = f32[1024,128]{1,0:T(8,128)} async-done(((f32[1024,4096]{1,0:T(8,128)}), f32[1024,128]{1,0:T(8,128)}) %reduce-scatter.2.cloned.1.call-update) | async-done | bytes 524304 | tf_op jit(solution)/shard_map/reduce_scatter | solution.py:110
  470.7 1.8 convert_element_type.67
  (26 shorter events, 3.2 us)
Async XLA Ops:
  6.5 293.5 %copy-start = (bf16[128,4096]{1,0:T(8,128)(2,1)S(1)}, bf16[128,4096]{1,0:T(8,128)(2,1)}, u32[]{:S(2)}) copy-start(bf16[128,4096]{1,0:T(8,128)(2,1)} %param.11) | copy-start | bytes 3145732
  12.0 193.7 %all-to-all-start = ((bf16[32,1024,128]{1,2,0:T(8,128)(2,1)}), bf16[32,1024,128]{1,2,0:T(8,128)(2,1)}, u32[]{:S(2)}, u32[]{:S(2)}) async-start(bf16[32,1024,128]{1,2,0:T(8,128)(2,1)} %stack.6), calls=%async_computation | async-start | bytes 16777216 | tf_op jit(solution)/shard_map/all_to_all | solution.py:10
  205.7 17.5 %copy-start.3 = (f32[3,3,128]{2,1,0:T(4,128)S(1)}, f32[3,3,128]{2,1,0:T(4,128)}, u32[]{:S(2)}) copy-start(f32[3,3,128]{2,1,0:T(4,128)} %param.8) | copy-start | bytes 13828
  205.7 17.6 %copy-start.2 = (f32[1024,128]{1,0:T(8,128)S(1)}, f32[1024,128]{1,0:T(8,128)}, u32[]{:S(2)}) copy-start(f32[1024,128]{1,0:T(8,128)} %param.9) | copy-start | bytes 1572868
  214.6 9.9 %collective-permute-start = (bf16[2,3,128]{2,1,0:T(4,128)(2,1)S(1)}, bf16[2,3,128]{2,1,0:T(4,128)(2,1)S(1)}, u32[]{:S(2)}, u32[]{:S(2)}) collective-permute-start(bf16[2,3,128]{2,1,0:T(4,128)(2,1)S(1)} %slice.51), channel_id=1, source_target_pairs={{0,32},{32,64},{64,96},{96,128},{128,160},{160,192},{192,224},{1,3... | collective-permute-start | bytes 4616 | tf_op jit(solution)/shard_map/ppermute | solution.py:17
  228.2 18.3 %all-to-all-start.1 = ((f32[2,1024,128]{1,0,2:T(2,128)}), f32[2,1024,128]{1,0,2:T(2,128)}, u32[]{:S(2)}, u32[]{:S(2)}) async-start(f32[2,1024,128]{1,0,2:T(2,128)} %copy.35), calls=%async_computation.1 | async-start | bytes 2097152 | tf_op jit(solution)/shard_map/all_to_all | solution.py:63
  234.8 235.9 %reduce-scatter.2.cloned.1.call-start = ((), (), s32[]{:S(2)}) async-start(), calls=%async_computation.4 | async-start | bytes 17301504 | tf_op jit(solution)/shard_map/reduce_scatter | solution.py:110
  252.2 3.2 copy-start.1
  285.8 14.1 %copy-start.4 = (f32[128]{0:T(128)S(1)}, f32[128]{0:T(128)}, u32[]{:S(2)}) copy-start(f32[128]{0:T(128)} %param.10) | copy-start | bytes 1540
Sparse Core Ops, SparseCore 0:
  308.3 162.3 reduce-scatter.1
